TPU v7x, 32 devices: a whole 2x2x4 slice. The times are simulated.
32 devices in a mesh: req: 8 (over z, y), tp: 4 (over x, core).
Axes of the slice: x: 2, y: 2, z: 4, core: 2. Of those that a mesh axis runs over, the one named last changes fastest.
Arguments:
- tokens_in: bfloat16 [24, 4, 2048], P('req'), may hold values from -6 to 6
- attn_norm: bfloat16 [2048], replicated, may hold values from 0.099609375 to 1.8984375
- qkv_weight: bfloat16 [2048, 3, 2048], P(None, None, 'tp'), may hold values from -0.125 to 0.125
- qkv_bias: bfloat16 [3, 2048], P(None, 'tp'), may hold values from -12 to 12
- out_weight: bfloat16 [2048, 2048], P('tp'), may hold values from -0.125 to 0.125
- cache_keys: bfloat16 [320, 128, 2048], P('req', None, 'tp'), may hold values from -12 to 12
- cache_values: bfloat16 [320, 128, 2048], P('req', None, 'tp'), may hold values from -6 to 6
- page_table: int32 [24, 37], replicated, may hold values from -1 to 319, as said below
- cache_lengths: int32 [24], replicated, may hold values from 1 to 4736, as said below
- mlp_norm: bfloat16 [2048], replicated, may hold values from 0.099609375 to 1.8984375
- routes: int32 [24, 4, 4], P('req'), may hold values from 0 to 7, all different within a row; in each aligned block of 12 rows (0 to 11, 12 to 23, ..., all dimensions but the last counted through in order) at most 6 rows name the same one
- route_gates: float32 [24, 4, 4], P('req'), may hold values from 0.05 to 0.5
- expert_w_gate: bfloat16 [8, 2048, 1408], P('req', None, 'tp'), may hold values from -0.125 to 0.125
- expert_w_up: bfloat16 [8, 2048, 1408], P('req', None, 'tp'), may hold values from -0.125 to 0.125
- expert_w_down: bfloat16 [8, 1408, 2048], P('req', 'tp'), may hold values from -0.15625 to 0.15625
- shared_w_gate: bfloat16 [2048, 5632], P('tp', 'req'), may hold values from -0.125 to 0.125
- shared_w_up: bfloat16 [2048, 5632], P('tp', 'req'), may hold values from -0.125 to 0.125
- shared_w_down: bfloat16 [5632, 2048], P('req', 'tp'), may hold values from -0.078125 to 0.078125
- shared_switch: bfloat16 [2048], replicated, may hold values from -0.125 to 0.125
Outputs:
- layer_out: bfloat16 [24, 4, 2048], P('req', None, 'tp')
Inputs may be any that keep to these rules, and one draw needn't show every extreme that they name: `page_table`: entry [r, j] is the pool page holding positions j*128 to (j+1)*128 - 1 of request r's cache, or -1. No pool page is named twice. 6 requests, drawn from the seed, have all 37 entries set, all outside the first 12 pages of every block of 40 pool pages; every other request r has exactly its first 4 entries set, all among pool pages (r // 3)*40 to (r // 3)*40 + 3*4 - 1. `cache_lengths`: A long request has 2368 to 4736 cached tokens, any other 1 to 512; both largest values occur in every draw. `routes`: the 4 experts of a token differ. Among the 12 tokens of each aligned block of rows (those of one index of req) no expert is named more than 6 times, and in some of those blocks one expert is named exactly 6 times.
All inputs are finite; a program needn't handle non-finite values.
Results may differ from a plain program's by a relative error of at most 0.006.
Values may be sent and summed in bfloat16 or wider, within the bound.
No kernel may reach another device: no remote copies, remote signals or barrier semaphores. Data moves between devices by JAX's collectives and lax.ppermute only.
A program may use at most 128 MiB of HBM per device.

v0:
```python
import math
import jax
import jax.numpy as jnp
from jax import lax
from jax.sharding import PartitionSpec as P

HD = 128
TOPK = 4
NEG = -1e30
EPS = 1e-06
THETA = 1000000.0
HIGHEST = lax.Precision.HIGHEST


def rms_norm(inputs, gain_vector):
    values = inputs.astype(jnp.float32)
    scaled = values * lax.rsqrt(jnp.mean(values * values, axis=-1, keepdims=True) + EPS)
    return (scaled * gain_vector.astype(jnp.float32)).astype(jnp.bfloat16)


def rotate(values, positions):
    half_dim = values.shape[-1] // 2
    exponents = jnp.arange(half_dim, dtype=jnp.float32) * (2.0 / values.shape[-1])
    frequency = jnp.power(THETA, -exponents)
    angles = positions.astype(jnp.float32)[..., None, None] * frequency
    cosines = jnp.cos(angles)
    sine_part = jnp.sin(angles)
    front_half = values[..., :half_dim]
    back_half = values[..., half_dim:]
    return jnp.concatenate(
        [
            front_half * cosines - back_half * sine_part,
            back_half * cosines + front_half * sine_part,
        ],
        axis=-1,
    )


def per_device(
    tokens_in,
    attn_norm,
    qkv_weight,
    qkv_bias,
    out_weight,
    cache_keys,
    cache_values,
    page_table,
    cache_lengths,
    mlp_norm,
    routes,
    route_gates,
    expert_w_gate,
    expert_w_up,
    expert_w_down,
    shared_w_gate,
    shared_w_up,
    shared_w_down,
    shared_switch,
):
    req_rows, step_count, model_width = tokens_in.shape
    head_width = qkv_weight.shape[2]
    local_heads = head_width // HD
    req_count = lax.axis_size("req")
    tp_count = lax.axis_size("tp")
    req_index = lax.axis_index("req")
    tp_index = lax.axis_index("tp")
    all_requests = page_table.shape[0]
    pool_here = cache_keys.shape[0]
    page_len = cache_keys.shape[1]
    score_scale = 1.0 / math.sqrt(HD)
    col_share = model_width // tp_count
    row_count = req_rows * step_count
    normed = rms_norm(tokens_in, attn_norm)
    projected = jnp.einsum(
        "rsd,dcf->rscf", normed, qkv_weight, preferred_element_type=jnp.float32
    ) + qkv_bias.astype(jnp.float32)
    own_lengths = lax.dynamic_slice_in_dim(cache_lengths, req_index * req_rows, req_rows)
    positions = own_lengths[:, None] + jnp.arange(step_count, dtype=jnp.int32)[None, :]
    head_shape = (req_rows, step_count, local_heads, HD)
    query_new = rotate(projected[:, :, 0].reshape(head_shape), positions).astype(jnp.bfloat16)
    key_new = rotate(projected[:, :, 1].reshape(head_shape), positions).astype(jnp.bfloat16)
    value_new = projected[:, :, 2].reshape(head_shape).astype(jnp.bfloat16)
    query_all = lax.all_gather(query_new, "req", axis=0, tiled=True)
    slot_ids = req_index * pool_here + jnp.arange(pool_here, dtype=jnp.int32)
    matches = (page_table[:, :, None] == slot_ids[None, None, :]).astype(jnp.int32)
    request_ids = jnp.arange(all_requests, dtype=jnp.int32)
    page_ids = jnp.arange(page_table.shape[1], dtype=jnp.int32)
    owner = jnp.sum(matches * request_ids[:, None, None], axis=(0, 1))
    logical = jnp.sum(matches * page_ids[None, :, None], axis=(0, 1))
    present = jnp.sum(matches, axis=(0, 1)) > 0
    token_pos = logical[:, None] * page_len + jnp.arange(page_len, dtype=jnp.int32)[None, :]
    live = present[:, None] & (token_pos < cache_lengths[owner][:, None])
    page_queries = query_all[owner]
    page_keys = cache_keys.reshape(pool_here, page_len, local_heads, HD)
    page_values = cache_values.reshape(pool_here, page_len, local_heads, HD)
    scores = (
        jnp.einsum("pshd,pkhd->pshk", page_queries, page_keys, preferred_element_type=jnp.float32)
        * score_scale
    )
    page_mask = live[:, None, None, :]
    masked = jnp.where(page_mask, scores, NEG)
    page_max = jnp.max(masked, axis=-1)
    weights = jnp.where(page_mask, jnp.exp(masked - page_max[..., None]), 0.0)
    page_sum = jnp.sum(weights, axis=-1)
    page_out = jnp.einsum(
        "pshk,pkhd->pshd",
        weights.astype(jnp.bfloat16),
        page_values,
        preferred_element_type=jnp.float32,
    )
    belongs = (owner[None, :] == request_ids[:, None]) & present[None, :]
    owned = belongs[:, :, None, None]
    local_max = jnp.max(jnp.where(owned, page_max[None], NEG), axis=1)
    factors = jnp.where(owned, jnp.exp(page_max[None] - local_max[:, None]), 0.0)
    local_out = jnp.einsum("rpsh,pshd->rshd", factors, page_out, precision=HIGHEST)
    local_sum = jnp.einsum("rpsh,psh->rsh", factors, page_sum, precision=HIGHEST)
    first_row = req_index * req_rows
    global_max = lax.pmax(local_max, "req")
    rescale = jnp.exp(local_max - global_max)
    summed_out, summed_sum = lax.psum((local_out * rescale[..., None], local_sum * rescale), "req")
    cache_max = lax.dynamic_slice_in_dim(global_max, first_row, req_rows)
    cache_out = lax.dynamic_slice_in_dim(summed_out, first_row, req_rows)
    cache_sum = lax.dynamic_slice_in_dim(summed_sum, first_row, req_rows)
    new_scores = (
        jnp.einsum("rshd,rthd->rsht", query_new, key_new, preferred_element_type=jnp.float32)
        * score_scale
    )
    causal = jnp.arange(step_count)[:, None] >= jnp.arange(step_count)[None, :]
    new_mask = causal[None, :, None, :]
    new_masked = jnp.where(new_mask, new_scores, NEG)
    new_max = jnp.max(new_masked, axis=-1)
    new_weights = jnp.where(new_mask, jnp.exp(new_masked - new_max[..., None]), 0.0)
    new_sum = jnp.sum(new_weights, axis=-1)
    new_out = jnp.einsum(
        "rsht,rthd->rshd",
        new_weights.astype(jnp.bfloat16),
        value_new,
        preferred_element_type=jnp.float32,
    )
    top_max = jnp.maximum(cache_max, new_max)
    cache_factor = jnp.exp(cache_max - top_max)
    new_factor = jnp.exp(new_max - top_max)
    attended = (cache_out * cache_factor[..., None] + new_out * new_factor[..., None]) / (
        cache_sum * cache_factor + new_sum * new_factor
    )[..., None]
    attended = attended.astype(jnp.bfloat16).reshape(row_count, head_width)
    attn_part = jnp.dot(attended, out_weight, preferred_element_type=jnp.float32)
    attn_full = lax.psum(attn_part, "tp")
    resid = tokens_in.reshape(row_count, model_width).astype(jnp.float32) + attn_full
    mixed = rms_norm(resid, mlp_norm)
    expert_count = req_count * expert_w_gate.shape[0]
    capacity = max(2, (row_count * TOPK + expert_count - 1) // expert_count)
    picks = routes.reshape(row_count * TOPK)
    gates_flat = route_gates.reshape(row_count * TOPK)
    expert_hot = (picks[:, None] == jnp.arange(expert_count, dtype=jnp.int32)[None, :]).astype(
        jnp.int32
    )
    slot_index = jnp.sum((jnp.cumsum(expert_hot, axis=0) - 1) * expert_hot, axis=1)
    destination = picks * capacity + slot_index
    dest_hot = (
        destination[:, None] == jnp.arange(expert_count * capacity, dtype=jnp.int32)[None, :]
    ).astype(jnp.float32)
    token_hot = (
        (jnp.arange(row_count * TOPK, dtype=jnp.int32) // TOPK)[:, None]
        == jnp.arange(row_count, dtype=jnp.int32)[None, :]
    ).astype(jnp.float32)
    placement = jnp.einsum("cx,ct->xt", dest_hot, token_hot, precision=HIGHEST).astype(jnp.bfloat16)
    outgoing = jnp.dot(placement, mixed, preferred_element_type=jnp.float32).astype(jnp.bfloat16)
    outgoing = outgoing.reshape(expert_count, capacity, model_width)
    combine_map = jnp.einsum(
        "ct,cx->tx", token_hot, dest_hot * gates_flat[:, None], precision=HIGHEST
    )
    w_gate_here = expert_w_gate[0]
    w_up_here = expert_w_up[0]
    w_down_here = expert_w_down[0]
    received = lax.all_to_all(outgoing, "req", split_axis=0, concat_axis=0, tiled=True)
    sources = received.shape[0]
    item_count = received.shape[1]
    flat_rows = received.reshape(sources * item_count, model_width)
    gate_pre = jnp.dot(flat_rows, w_gate_here, preferred_element_type=jnp.float32)
    up_pre = jnp.dot(flat_rows, w_up_here, preferred_element_type=jnp.float32)
    hidden = (jax.nn.silu(gate_pre) * up_pre).astype(jnp.bfloat16)
    partial_out = jnp.dot(hidden, w_down_here, preferred_element_type=jnp.float32).reshape(
        sources, item_count, model_width
    )
    summed = lax.psum(partial_out, "tp").astype(jnp.bfloat16)
    returned = lax.all_to_all(summed, "req", split_axis=0, concat_axis=0, tiled=True)
    returned_cols = returned.shape[2]
    moe_out = jnp.dot(
        combine_map,
        returned.reshape(expert_count * capacity, returned_cols).astype(jnp.float32),
        precision=HIGHEST,
    )
    moe_out = lax.dynamic_slice_in_dim(moe_out, tp_index * col_share, col_share, 1)
    mixed_cols = lax.dynamic_slice_in_dim(mixed, tp_index * col_share, col_share, 1)
    piece = lax.all_gather(mixed_cols, "req", axis=0, tiled=True)
    gate_part = jnp.dot(piece, shared_w_gate, preferred_element_type=jnp.float32)
    up_part = jnp.dot(piece, shared_w_up, preferred_element_type=jnp.float32)
    shared_pre = jnp.concatenate([gate_part, up_part], axis=1)
    shared_pre = lax.psum(shared_pre, "tp")
    unit_count = shared_w_gate.shape[1]
    shared_hidden = (jax.nn.silu(shared_pre[:, :unit_count]) * shared_pre[:, unit_count:]).astype(
        jnp.bfloat16
    )
    shared_mine = lax.psum_scatter(
        jnp.dot(shared_hidden, shared_w_down, preferred_element_type=jnp.float32),
        "req",
        scatter_dimension=0,
        tiled=True,
    )
    switch = jax.nn.sigmoid(jnp.dot(mixed, shared_switch, preferred_element_type=jnp.float32))
    resid_mine = lax.dynamic_slice_in_dim(resid, tp_index * col_share, col_share, 1)
    final = resid_mine + moe_out + switch[:, None] * shared_mine
    return final.astype(jnp.bfloat16).reshape(req_rows, step_count, col_share)


def solution(mesh):
    return jax.shard_map(
        per_device,
        mesh=mesh,
        in_specs=(
            P("req", None, None),
            P(),
            P(None, None, "tp"),
            P(None, "tp"),
            P("tp", None),
            P("req", None, "tp"),
            P("req", None, "tp"),
            P(),
            P(),
            P(),
            P("req", None, None),
            P("req", None, None),
            P("req", None, "tp"),
            P("req", None, "tp"),
            P("req", "tp", None),
            P("tp", "req"),
            P("tp", "req"),
            P("req", "tp"),
            P(),
        ),
        out_specs=P("req", None, "tp"),
        check_vma=False,
    )
```

profile of v0, /device:TPU:0, one launch (start us, length us, event | category | flops | bytes accessed | tf_op | source)
XLA Modules:
  0.0 321.9 jit_solution(12219065390824033137)
XLA Ops:
  10.9 1.4 gather_fusion
  12.4 3.8 %fusion.28 = f32[3,4,3,512]{3,1,2,0:T(4,128)S(1)} fusion(bf16[2048,3,512]{2,0,1:T(8,128)(2,1)} %param.21, bf16[3,4,2048]{2,1,0:T(4,128)(2,1)} %param.19, f32[2048]{0:T(1024)S(1)} %convert_element_type.78, f32[3,4]{1,0:T(4,128)S(1)} %add_rsqrt_fusion, f32[3,512]{1,0:T(4,128)S(1)} %convert_element_type.80), kind=kOutput, calls=%fused_computation.23 | convolution fusion | flops 75614208 | bytes 6428720 | tf_op jit(solution)/shard_map/rsd,dcf->rscf/dot_general | solution.py:74
  17.7 32.3 %all_gather.6 = bf16[24,4,4,128]{3,2,1,0:T(4,128)(2,1)S(1)} all-gather(bf16[3,4,4,128]{3,2,1,0:T(4,128)(2,1)S(1)} %copy.91), channel_id=1, replica_groups=mesh['req'=8,'tp'=4] {'req'}, dimensions={0}, use_global_device_ids=true | all-gather | bytes 110592 | tf_op jit(solution)/shard_map/all_gather | solution.py:83
  50.8 5.4 %fusion.114 = (f32[40,4,4]{1,2,0:T(4,128)S(1)}, f32[40,4,4,128]{3,1,2,0:T(4,128)S(1)}) fusion(bf16[40,4,4,128]{3,2,1,0:T(4,128)(2,1)S(1)} %gather_fusion.1, pred[40,128]{1,0:T(8,128)(4,1)S(1)} %fusion.81, bf16[40,128,512]{2,1,0:T(8,128)(2,1)} %param.24), kind=kOutput, calls=%fused_computation.150 | convolution fusion | flops 21216640 | bytes 5742080 | tf_op jit(solution)/shard_map/pshd,pkhd->pshk/dot_general | solution.py:97
  56.5 22.2 %pmax.7 = f32[24,4,4]{0,2,1:T(4,128)} all-reduce(f32[24,4,4]{0,2,1:T(4,128)S(1)} %select_reduce_fusion), channel_id=1, replica_groups=mesh['req'=8,'tp'=4] {'req'}, use_global_device_ids=true, to_apply=%region_6.7 | all-reduce | flops 384 | bytes 3072 | tf_op jit(solution)/shard_map/pmax | solution.py:118
  79.8 4.1 %fusion.15 = f32[40,4,4,128]{3,1,2,0:T(4,128)S(1)} fusion(f32[40,4,4,128]{3,1,2,0:T(4,128)S(1)} %get-tuple-element.28, f32[40,4,4]{1,2,0:T(4,128)S(1)} %get-tuple-element.27, pred[40,128]{1,0:T(8,128)(4,1)} %copy-done.7, bf16[40,128,512]{2,1,0:T(8,128)(2,1)} %param.25), kind=kOutput, calls=%fused_computation.17 | convolution fusion | flops 21217280 | bytes 5905920 | tf_op jit(solution)/shard_map/pshk,pkhd->pshd/dot_general | solution.py:105
  86.9 2.0 fusion.21
  92.2 17.4 %psum.36 = f32[24,4,4]{0,2,1:T(4,128)S(1)} all-reduce(f32[24,4,4]{0,2,1:T(4,128)S(1)} %bitcast.134), channel_id=1, replica_groups=mesh['req'=8,'tp'=4] {'req'}, use_global_device_ids=true, to_apply=%region_10.11 | all-reduce | flops 384 | bytes 3072 | tf_op jit(solution)/shard_map/psum | solution.py:120
  110.4 46.0 %all-reduce.7.cloned.1.call-done = f32[24,4,4,128]{3,0,2,1:T(8,128)} async-done(((f32[24,4,4,128]{3,0,2,1:T(8,128)}), f32[24,4,4,128]{3,0,2,1:T(8,128)}) %all-reduce.7.cloned.1.call-update) | async-done | bytes 196624 | tf_op jit(solution)/shard_map/psum | solution.py:120
  161.1 28.1 %all-reduce.9.cloned.1.call-done = f32[12,2048]{1,0:T(8,128)} async-done(((f32[12,2048]{1,0:T(8,128)}), f32[12,2048]{1,0:T(8,128)}) %all-reduce.9.cloned.1.call-update) | async-done | bytes 98320 | tf_op jit(solution)/shard_map/psum | solution.py:148
  190.4 30.6 %all-gather = bf16[8,12,512]{2,1,0:T(8,128)(2,1)S(1)} all-gather(bf16[1,12,512]{2,1,0:T(8,128)(2,1)S(1)} %dynamic-slice_bitcast_fusion), channel_id=1, replica_groups=mesh['req'=8,'tp'=4] {'req'}, dimensions={0}, use_global_device_ids=true | all-gather | bytes 110592 | tf_op jit(solution)/shard_map/all_gather | solution.py:196
  221.4 1.5 fusion.117
  224.9 5.5 %all-to-all-start = ((bf16[8,6,2048]{2,1,0:T(8,128)(2,1)}), bf16[8,6,2048]{2,1,0:T(8,128)(2,1)S(1)}, u32[]{:S(2)}, u32[]{:S(2)}) async-start(bf16[8,6,2048]{2,1,0:T(8,128)(2,1)} %reshape.235), calls=%async_computation | async-start | bytes 524288 | tf_op jit(solution)/shard_map/all_to_all | solution.py:176
  231.9 25.2 %all-reduce.11.cloned.1.call-done = f32[96,1408]{1,0:T(8,128)} async-done(((f32[96,1408]{1,0:T(8,128)}), f32[96,1408]{1,0:T(8,128)}) %all-reduce.11.cloned.1.call-update) | async-done | bytes 540688 | tf_op jit(solution)/shard_map/psum | solution.py:200
  257.1 1.6 fusion.56
  258.7 1.9 fusion.13
  260.7 1.9 fusion.25
  262.6 1.7 fusion.9
  264.3 14.5 %all-reduce.12 = bf16[8,6,2048]{2,0,1:T(8,128)(2,1)S(1)} all-reduce(f32[8,6,2048]{2,0,1:T(8,128)S(1)} %fusion.9), channel_id=1, replica_groups=mesh['req'=8,'tp'=4] {'tp'}, use_global_device_ids=true, to_apply=%region_16.17 | all-reduce | flops 98304 | bytes 589824 | tf_op jit(solution)/shard_map/psum | solution.py:186
  279.6 5.4 %all-to-all-start.1 = ((bf16[8,6,2048]{2,1,0:T(8,128)(2,1)}), bf16[8,6,2048]{2,1,0:T(8,128)(2,1)S(1)}, u32[]{:S(2)}, u32[]{:S(2)}) async-start(bf16[8,6,2048]{2,1,0:T(8,128)(2,1)} %copy.108), calls=%async_computation.1 | async-start | bytes 524288 | tf_op jit(solution)/shard_map/all_to_all | solution.py:187
  285.1 24.1 %fusion = f32[16,512]{1,0:T(8,128)S(1)} fusion(f32[96,512]{1,0:T(8,128)S(1)} %fusion.56), kind=kCustom, calls=%all-reduce-scatter | all-reduce-scatter fusion | flops 65537 | bytes 229888
  309.2 2.1 collective-permute-start
  311.2 1.3 collective-permute-start.1
  312.7 1.4 collective-permute-done.1
  (100 shorter events, 26.4 us)
Async XLA Ops:
  6.5 150.9 %copy-start = (bf16[512,2048]{1,0:T(8,128)(2,1)S(1)}, bf16[512,2048]{1,0:T(8,128)(2,1)}, u32[]{:S(2)}) copy-start(bf16[512,2048]{1,0:T(8,128)(2,1)} %param.23) | copy-start | bytes 6291460
  6.5 149.8 %all-reduce.7.cloned.1.call-start = ((), (), s32[]{:S(2)}) async-start(), calls=%async_computation.2 | async-start | bytes 393216 | tf_op jit(solution)/shard_map/psum | solution.py:120
  10.9 45.4 %copy-start.6 = (pred[24,40]{1,0:T(8,128)(4,1)}, pred[24,40]{1,0:T(8,128)(4,1)S(1)}, u32[]{:S(2)}) copy-start(pred[24,40]{1,0:T(8,128)(4,1)S(1)} %fusion.98) | copy-start | bytes 2884
  16.2 0.9 copy-start.5
  17.1 0.6 copy-start.4
  50.8 27.9 %copy-start.7 = (pred[40,128]{1,0:T(8,128)(4,1)}, pred[40,128]{1,0:T(8,128)(4,1)S(1)}, u32[]{:S(2)}) copy-start(pred[40,128]{1,0:T(8,128)(4,1)S(1)} %fusion.81) | copy-start | bytes 15364
  56.3 22.3 %copy-start.3 = (f32[40,4,4]{0,2,1:T(4,128)}, f32[40,4,4]{0,2,1:T(4,128)S(1)}, u32[]{:S(2)}) copy-start(f32[40,4,4]{0,2,1:T(4,128)S(1)} %copy.96) | copy-start | bytes 7684
  56.5 22.2 %copy-start.2 = (f32[24,4,4]{0,2,1:T(4,128)}, f32[24,4,4]{0,2,1:T(4,128)S(1)}, u32[]{:S(2)}) copy-start(f32[24,4,4]{0,2,1:T(4,128)S(1)} %select_reduce_fusion) | copy-start | bytes 4612
  79.8 141.2 %copy-start.1 = (bf16[512,704]{0,1:T(8,128)(2,1)S(1)}, bf16[512,704]{0,1:T(8,128)(2,1)}, u32[]{:S(2)}) copy-start(bf16[512,704]{0,1:T(8,128)(2,1)} %param.35) | copy-start | bytes 2162692
  86.8 143.8 %copy-start.8 = (bf16[2048]{0:T(1024)(128)(2,1)S(1)}, bf16[2048]{0:T(1024)(128)(2,1)}, u32[]{:S(2)}) copy-start(bf16[2048]{0:T(1024)(128)(2,1)} %param.37) | copy-start | bytes 12292
  86.8 143.8 %copy-start.9 = (u32[32]{0:T(128)S(1)}, u32[32]{0:T(128)}, u32[]{:S(2)}) copy-start(u32[32]{0:T(128)} %constant.87) | copy-start | bytes 388
  88.9 100.4 %all-reduce.9.cloned.1.call-start = ((), (), s32[]{:S(2)}) async-start(), calls=%async_computation.3 | async-start | bytes 262144 | tf_op jit(solution)/shard_map/psum | solution.py:148
  158.5 98.5 %all-reduce.11.cloned.1.call-start = ((), (), s32[]{:S(2)}) async-start(), calls=%async_computation.4 | async-start | bytes 1081344 | tf_op jit(solution)/shard_map/psum | solution.py:200
  224.9 33.8 %all-to-all-start = ((bf16[8,6,2048]{2,1,0:T(8,128)(2,1)}), bf16[8,6,2048]{2,1,0:T(8,128)(2,1)S(1)}, u32[]{:S(2)}, u32[]{:S(2)}) async-start(bf16[8,6,2048]{2,1,0:T(8,128)(2,1)} %reshape.235), calls=%async_computation | async-start | bytes 524288 | tf_op jit(solution)/shard_map/all_to_all | solution.py:176
  279.6 34.7 %all-to-all-start.1 = ((bf16[8,6,2048]{2,1,0:T(8,128)(2,1)}), bf16[8,6,2048]{2,1,0:T(8,128)(2,1)S(1)}, u32[]{:S(2)}, u32[]{:S(2)}) async-start(bf16[8,6,2048]{2,1,0:T(8,128)(2,1)} %copy.108), calls=%async_computation.1 | async-start | bytes 524288 | tf_op jit(solution)/shard_map/all_to_all | solution.py:187
  309.2 4.9 %collective-permute-start = (f32[16,512]{1,0:T(8,128)S(1)}, f32[16,512]{1,0:T(8,128)S(1)}, u32[]{:S(2)}, u32[]{:S(2)}) collective-permute-start(f32[16,512]{1,0:T(8,128)S(1)} %fusion), channel_id=1, source_target_pairs={{0,4},{4,8},{8,12},{12,16},{16,20},{20,24},{24,28},{1,5},{5,9},{9,... | collective-permute-start | bytes 98312
  311.2 2.9 collective-permute-start.1
Sparse Core Ops, SparseCore 0:
  89.0 67.3 all-reduce.6
  158.8 30.4 all-reduce.8
  224.0 33.0 all-reduce.10
where the time goes:
time: 323 us; the launch traced here: 322 us
  blocking collectives  141 us (44%)
  waiting for transfers between devices  101 us (31%)
  matrix products  29.5 us (9%)
  starting transfers between devices  14.3 us (4%)
  between operations  14.2 us (4%)
  local copies, waits for them, and re-layouts  11.4 us (4%)
  other arithmetic  10.7 us (3%)
    psum x1, waiting for transfers between devices, per_device(): lax.psum((local_out * rescale[..., None], local_sum * rescale), 'req')  46 us
    all_gather x1, blocking collectives, per_device(): query_all = lax.all_gather(query_new, 'req', axis=0, tiled=True)  32.3 us
    all_gather x1, blocking collectives, per_device(): piece = lax.all_gather(mixed_cols, 'req', axis=0, tiled=True)  30.6 us
    psum x1, waiting for transfers between devices, per_device(): attn_full = lax.psum(attn_part, 'tp')  28.1 us
    psum x1, waiting for transfers between devices, per_device(): shared_pre = lax.psum(shared_pre, 'tp')  25.2 us
    unnamed x1, blocking collectives  24.1 us
    pmax x1, blocking collectives, per_device(): global_max = lax.pmax(local_max, 'req')  22.2 us
    psum x1, blocking collectives, per_device(): lax.psum((local_out * rescale[..., None], local_sum * rescale), 'req')  17.4 us
  transfers between devices with their start and end apart: 7, of which 4 were waited for; matrix products, arithmetic and copies ran while one was open for 11% of the time, Pallas kernels for 0%

commit v1 on v0

--- a/solution.py
+++ b/solution.py
@@ -197,7 +197,7 @@
     gate_part = jnp.dot(piece, shared_w_gate, preferred_element_type=jnp.float32)
     up_part = jnp.dot(piece, shared_w_up, preferred_element_type=jnp.float32)
     shared_pre = jnp.concatenate([gate_part, up_part], axis=1)
-    shared_pre = lax.psum(shared_pre, "tp")
+    shared_pre = jnp.sum(lax.all_gather(shared_pre, "tp"), axis=0)
     unit_count = shared_w_gate.shape[1]
     shared_hidden = (jax.nn.silu(shared_pre[:, :unit_count]) * shared_pre[:, unit_count:]).astype(
         jnp.bfloat16

time: 323 us -> 307 us (0.950)
  waiting for transfers between devices: 101 us -> 95 us
  local copies, waits for them, and re-layouts: 11.4 us -> 7.73 us
    psum x1 -> x0, waiting for transfers between devices: 25.2 us -> none  [per_device(): shared_pre = lax.psum(shared_pre, 'tp')]
    all_to_all x1, waiting for transfers between devices: 0.01 us -> 7.76 us  [per_device(): lax.all_to_all(summed, 'req', split_axis=0, concat_axis=0, tiled=True)]
    all_to_all x1, waiting for transfers between devices: 0.01 us -> 6.85 us  [per_device(): lax.all_to_all(outgoing, 'req', split_axis=0, concat_axis=0, tiled=True)]
  transfers between devices with their start and end apart: 7 -> 7, of which waited for: 4 -> 5; matrix products, arithmetic and copies ran while one was open for 11% -> 4% of each run, Pallas kernels for 0% -> 0%
where the time goes in v1:
time: 307 us; the launch traced here: 306 us
  blocking collectives  139 us (45%)
  waiting for transfers between devices  95 us (31%)
  matrix products  26.7 us (9%)
  between operations  14.2 us (5%)
  starting transfers between devices  12.3 us (4%)
  other arithmetic  10.6 us (3%)
  local copies, waits for them, and re-layouts  7.73 us (3%)
    psum x1, waiting for transfers between devices, per_device(): lax.psum((local_out * rescale[..., None], local_sum * rescale), 'req')  49 us
    all_gather x1, blocking collectives, per_device(): query_all = lax.all_gather(query_new, 'req', axis=0, tiled=True)  32.3 us
    all_gather x1, blocking collectives, per_device(): piece = lax.all_gather(mixed_cols, 'req', axis=0, tiled=True)  30.6 us
    psum x1, waiting for transfers between devices, per_device(): attn_full = lax.psum(attn_part, 'tp')  30 us
    unnamed x1, blocking collectives  22.6 us
    pmax x1, blocking collectives, per_device(): global_max = lax.pmax(local_max, 'req')  21.6 us
    psum x1, blocking collectives, per_device(): lax.psum((local_out * rescale[..., None], local_sum * rescale), 'req')  17.6 us
    psum x1, blocking collectives, per_device(): summed = lax.psum(partial_out, 'tp').astype(jnp.bfloat16)  14.5 us
  transfers between devices with their start and end apart: 7, of which 5 were waited for; matrix products, arithmetic and copies ran while one was open for 4% of the time, Pallas kernels for 0%

profile of v1, /device:TPU:0, one launch (start us, length us, event | category | flops | bytes accessed | tf_op | source)
XLA Modules:
  0.0 305.8 jit_solution(15455347939930904715)
XLA Ops:
  10.9 1.4 gather_fusion
  12.3 3.8 %fusion.28 = f32[3,4,3,512]{3,1,2,0:T(4,128)S(1)} fusion(bf16[2048,3,512]{2,0,1:T(8,128)(2,1)} %param.21, bf16[3,4,2048]{2,1,0:T(4,128)(2,1)} %param.19, f32[2048]{0:T(1024)S(1)} %convert_element_type.78, f32[3,4]{1,0:T(4,128)S(1)} %add_rsqrt_fusion, f32[3,512]{1,0:T(4,128)S(1)} %convert_element_type.80), kind=kOutput, calls=%fused_computation.23 | convolution fusion | flops 75614208 | bytes 6428720 | tf_op jit(solution)/shard_map/rsd,dcf->rscf/dot_general | solution.py:74
  16.5 32.3 %all_gather.12 = bf16[24,4,4,128]{3,2,1,0:T(4,128)(2,1)S(1)} all-gather(bf16[3,4,4,128]{3,2,1,0:T(4,128)(2,1)S(1)} %copy.91), channel_id=1, replica_groups=mesh['req'=8,'tp'=4] {'req'}, dimensions={0}, use_global_device_ids=true | all-gather | bytes 110592 | tf_op jit(solution)/shard_map/all_gather | solution.py:83
  49.6 5.4 %fusion.114 = (f32[40,4,4]{1,2,0:T(4,128)S(1)}, f32[40,4,4,128]{3,1,2,0:T(4,128)S(1)}) fusion(bf16[40,4,4,128]{3,2,1,0:T(4,128)(2,1)S(1)} %gather_fusion.1, pred[40,128]{1,0:T(8,128)(4,1)S(1)} %fusion.81, bf16[40,128,512]{2,1,0:T(8,128)(2,1)} %param.24), kind=kOutput, calls=%fused_computation.150 | convolution fusion | flops 21216640 | bytes 5742080 | tf_op jit(solution)/shard_map/pshd,pkhd->pshk/dot_general | solution.py:97
  55.3 21.6 %pmax.7 = f32[24,4,4]{0,2,1:T(4,128)S(1)} all-reduce(f32[24,4,4]{0,2,1:T(4,128)S(1)} %select_reduce_fusion), channel_id=1, replica_groups=mesh['req'=8,'tp'=4] {'req'}, use_global_device_ids=true, to_apply=%region_6.7 | all-reduce | flops 384 | bytes 3072 | tf_op jit(solution)/shard_map/pmax | solution.py:118
  77.5 4.2 %fusion.15 = f32[40,4,4,128]{3,1,2,0:T(4,128)S(1)} fusion(f32[40,4,4,128]{3,1,2,0:T(4,128)} %copy-done.2, f32[40,4,4]{1,2,0:T(4,128)S(1)} %get-tuple-element.27, pred[40,128]{1,0:T(8,128)(4,1)S(1)} %fusion.81, bf16[40,128,512]{2,1,0:T(8,128)(2,1)} %param.25), kind=kOutput, calls=%fused_computation.17 | convolution fusion | flops 21217280 | bytes 5905920 | tf_op jit(solution)/shard_map/pshk,pkhd->pshd/dot_general | solution.py:105
  84.3 17.6 %psum.29 = f32[24,4,4]{0,2,1:T(4,128)S(1)} all-reduce(f32[24,4,4]{0,2,1:T(4,128)S(1)} %bitcast.136), channel_id=1, replica_groups=mesh['req'=8,'tp'=4] {'req'}, use_global_device_ids=true, to_apply=%region_10.11 | all-reduce | flops 384 | bytes 3072 | tf_op jit(solution)/shard_map/psum | solution.py:120
  102.0 49.0 %all-reduce.6.cloned.1.call-done = f32[24,4,4,128]{3,0,2,1:T(8,128)} async-done(((f32[24,4,4,128]{3,0,2,1:T(8,128)}), f32[24,4,4,128]{3,0,2,1:T(8,128)}) %all-reduce.6.cloned.1.call-update) | async-done | bytes 196624 | tf_op jit(solution)/shard_map/psum | solution.py:120
  154.0 30.0 %all-reduce.8.cloned.1.call-done = f32[12,2048]{1,0:T(8,128)} async-done(((f32[12,2048]{1,0:T(8,128)}), f32[12,2048]{1,0:T(8,128)}) %all-reduce.8.cloned.1.call-update) | async-done | bytes 98320 | tf_op jit(solution)/shard_map/psum | solution.py:148
  185.1 30.6 %all-gather.1 = bf16[8,12,512]{2,1,0:T(8,128)(2,1)S(1)} all-gather(bf16[1,12,512]{2,1,0:T(8,128)(2,1)S(1)} %dynamic-slice_bitcast_fusion), channel_id=1, replica_groups=mesh['req'=8,'tp'=4] {'req'}, dimensions={0}, use_global_device_ids=true | all-gather | bytes 110592 | tf_op jit(solution)/shard_map/all_gather | solution.py:196
  216.1 1.5 fusion.117
  220.2 5.5 %all-to-all-start = ((bf16[8,6,2048]{2,1,0:T(8,128)(2,1)}), bf16[8,6,2048]{2,1,0:T(8,128)(2,1)S(1)}, u32[]{:S(2)}, u32[]{:S(2)}) async-start(bf16[8,6,2048]{2,1,0:T(8,128)(2,1)} %reshape.235), calls=%async_computation | async-start | bytes 524288 | tf_op jit(solution)/shard_map/all_to_all | solution.py:176
  227.1 6.8 %all-to-all-done = bf16[8,6,2048]{2,1,0:T(8,128)(2,1)S(1)} async-done(((bf16[8,6,2048]{2,1,0:T(8,128)(2,1)}), bf16[8,6,2048]{2,1,0:T(8,128)(2,1)S(1)}, u32[]{:S(2)}, u32[]{:S(2)}) %all-to-all-start) | async-done | bytes 196640 | tf_op jit(solution)/shard_map/all_to_all | solution.py:176
  234.0 1.9 fusion.13
  235.9 1.9 fusion.25
  237.9 1.7 fusion.9
  239.6 14.5 %all-reduce.9 = bf16[8,6,2048]{2,0,1:T(8,128)(2,1)S(1)} all-reduce(f32[8,6,2048]{2,0,1:T(8,128)S(1)} %fusion.9), channel_id=1, replica_groups=mesh['req'=8,'tp'=4] {'tp'}, use_global_device_ids=true, to_apply=%region_16.17 | all-reduce | flops 98304 | bytes 589824 | tf_op jit(solution)/shard_map/psum | solution.py:186
  254.9 3.4 %all-to-all-start.1 = ((bf16[8,6,2048]{2,1,0:T(8,128)(2,1)}), bf16[8,6,2048]{2,1,0:T(8,128)(2,1)S(1)}, u32[]{:S(2)}, u32[]{:S(2)}) async-start(bf16[8,6,2048]{2,1,0:T(8,128)(2,1)} %copy.108), calls=%async_computation.1 | async-start | bytes 524288 | tf_op jit(solution)/shard_map/all_to_all | solution.py:187
  258.7 7.8 %all-to-all-done.1 = bf16[8,6,2048]{2,1,0:T(8,128)(2,1)S(1)} async-done(((bf16[8,6,2048]{2,1,0:T(8,128)(2,1)}), bf16[8,6,2048]{2,1,0:T(8,128)(2,1)S(1)}, u32[]{:S(2)}, u32[]{:S(2)}) %all-to-all-start.1) | async-done | bytes 196640 | tf_op jit(solution)/shard_map/all_to_all | solution.py:187
  266.6 2.6 reduce_sum.92
  269.2 1.6 fusion.56
  270.7 22.6 %fusion = f32[16,512]{1,0:T(8,128)S(1)} fusion(f32[96,512]{1,0:T(8,128)S(1)} %fusion.56), kind=kCustom, calls=%all-reduce-scatter | all-reduce-scatter fusion | flops 65537 | bytes 229888
  293.4 2.1 collective-permute-start
  297.0 1.4 collective-permute-done.1
  (97 shorter events, 20.5 us)
Async XLA Ops:
  6.5 145.6 %copy-start = (bf16[512,2048]{1,0:T(8,128)(2,1)S(1)}, bf16[512,2048]{1,0:T(8,128)(2,1)}, u32[]{:S(2)}) copy-start(bf16[512,2048]{1,0:T(8,128)(2,1)} %param.23) | copy-start | bytes 6291460
  6.5 144.5 %all-reduce.6.cloned.1.call-start = ((), (), s32[]{:S(2)}) async-start(), calls=%async_computation.2 | async-start | bytes 393216 | tf_op jit(solution)/shard_map/psum | solution.py:120
  55.0 21.9 %copy-start.2 = (f32[40,4,4,128]{3,1,2,0:T(4,128)}, f32[40,4,4,128]{3,1,2,0:T(4,128)S(1)}, u32[]{:S(2)}) copy-start(f32[40,4,4,128]{3,1,2,0:T(4,128)S(1)} %get-tuple-element.28) | copy-start | bytes 983044
  77.4 75.8 %copy-start.3 = (bf16[3,4,2048]{2,1,0:T(4,128)(2,1)S(1)}, bf16[3,4,2048]{2,1,0:T(4,128)(2,1)}, u32[]{:S(2)}) copy-start(bf16[3,4,2048]{2,1,0:T(4,128)(2,1)} %param.19) | copy-start | bytes 147460
  77.4 138.3 %copy-start.1 = (bf16[512,704]{0,1:T(8,128)(2,1)S(1)}, bf16[512,704]{0,1:T(8,128)(2,1)}, u32[]{:S(2)}) copy-start(bf16[512,704]{0,1:T(8,128)(2,1)} %param.35) | copy-start | bytes 2162692
  81.6 136.9 %copy-start.4 = (s32[3,4,4]{2,1,0:T(4,128)S(1)}, s32[3,4,4]{2,1,0:T(4,128)}, u32[]{:S(2)}) copy-start(s32[3,4,4]{2,1,0:T(4,128)} %param.29) | copy-start | bytes 580
  82.3 143.4 %copy-start.5 = (f32[3,4,4]{2,1,0:T(4,128)S(1)}, f32[3,4,4]{2,1,0:T(4,128)}, u32[]{:S(2)}) copy-start(f32[3,4,4]{2,1,0:T(4,128)} %param.30) | copy-start | bytes 580
  82.3 143.5 %copy-start.6 = (bf16[2048]{0:T(1024)(128)(2,1)S(1)}, bf16[2048]{0:T(1024)(128)(2,1)}, u32[]{:S(2)}) copy-start(bf16[2048]{0:T(1024)(128)(2,1)} %param.37) | copy-start | bytes 12292
  82.3 143.5 %copy-start.7 = (u32[32]{0:T(128)S(1)}, u32[32]{0:T(128)}, u32[]{:S(2)}) copy-start(u32[32]{0:T(128)} %constant.87) | copy-start | bytes 388
  83.6 100.4 %all-reduce.8.cloned.1.call-start = ((), (), s32[]{:S(2)}) async-start(), calls=%async_computation.3 | async-start | bytes 262144 | tf_op jit(solution)/shard_map/psum | solution.py:148
  153.2 113.4 %all-gather.4.cloned.1.call-start = ((), (), s32[]{:S(2)}) async-start(), calls=%async_computation.4 | async-start | bytes 2703360 | tf_op jit(solution)/shard_map/all_gather | solution.py:200
  220.2 13.7 %all-to-all-start = ((bf16[8,6,2048]{2,1,0:T(8,128)(2,1)}), bf16[8,6,2048]{2,1,0:T(8,128)(2,1)S(1)}, u32[]{:S(2)}, u32[]{:S(2)}) async-start(bf16[8,6,2048]{2,1,0:T(8,128)(2,1)} %reshape.235), calls=%async_computation | async-start | bytes 524288 | tf_op jit(solution)/shard_map/all_to_all | solution.py:176
  254.9 11.6 %all-to-all-start.1 = ((bf16[8,6,2048]{2,1,0:T(8,128)(2,1)}), bf16[8,6,2048]{2,1,0:T(8,128)(2,1)S(1)}, u32[]{:S(2)}, u32[]{:S(2)}) async-start(bf16[8,6,2048]{2,1,0:T(8,128)(2,1)} %copy.108), calls=%async_computation.1 | async-start | bytes 524288 | tf_op jit(solution)/shard_map/all_to_all | solution.py:187
  293.4 5.0 %collective-permute-start = (f32[16,512]{1,0:T(8,128)S(1)}, f32[16,512]{1,0:T(8,128)S(1)}, u32[]{:S(2)}, u32[]{:S(2)}) collective-permute-start(f32[16,512]{1,0:T(8,128)S(1)} %fusion), channel_id=1, source_target_pairs={{0,4},{4,8},{8,12},{12,16},{16,20},{20,24},{24,28},{1,5},{5,9},{9,... | collective-permute-start | bytes 98312
  295.5 2.9 collective-permute-start.1
Sparse Core Ops, SparseCore 0:
  83.7 67.3 all-reduce.5
  153.5 30.4 all-reduce.7
  218.7 22.9 all-gather.3
